TPU v7x, 512 devices: a whole 4x8x8 slice. The times are simulated.
512 devices in a mesh: ctx: 32 (over z, x), tp: 16 (over y, core).
Axes of the slice: x: 4, y: 8, z: 8, core: 2. Of those that a mesh axis runs over, the one named last changes fastest.
Arguments:
- hidden: bfloat16 [8192, 2048], P(('ctx', 'tp')), may hold values from -14 to 14
- in_weight: bfloat16 [2048, 2, 4096], P(None, None, 'tp'), may hold values from -0.125 to 0.125
- step_weight: bfloat16 [2048, 64], P(None, 'tp'), may hold values from -0.125 to 0.125
- group_weight: bfloat16 [256, 4, 2048], P('tp'), may hold values from -0.125 to 0.125
- conv_inner: float32 [4, 4096], P(None, 'tp'), may hold values from -3 to 3
- inner_bias: float32 [4096], P('tp'), may hold values from -2.5 to 2.5
- conv_group: float32 [4, 1024], replicated, may hold values from -3 to 3
- group_bias: float32 [1024], replicated, may hold values from -2.5 to 2.5
- step_bias: float32 [64], P('tp'), may hold values from -9.5 to 0
- log_rate: float32 [64], P('tp'), may hold values from -2.5 to -0.5
- skip_weight: float32 [64], P('tp'), may hold values from 0.25 to 1
- norm_gain: float32 [4096], P('tp'), may hold values from 0.1 to 1.9
- out_weight: bfloat16 [4096, 2048], P('tp'), may hold values from -0.09375 to 0.09375
Outputs:
- mixed: bfloat16 [8192, 2048], P(('ctx', 'tp'))
All inputs are finite; a program needn't handle non-finite values.
Results may differ from a plain program's by a relative error of at most 0.024.
Values may be sent and summed in bfloat16 or wider, within the bound.
No kernel may reach another device: no remote copies, remote signals or barrier semaphores. Data moves between devices by JAX's collectives and lax.ppermute only.
A program may use at most 64 MiB of HBM per device.

v0:
```python
import jax
import jax.numpy as jnp
from jax import lax
from jax.sharding import PartitionSpec as P

HEADS = 64
HEAD_DIM = 64
STATE = 128
GROUPS = 4
BLOCK = 256
KERNEL = 4


def shifted(x, axis, by):
    peers = lax.axis_size(axis)
    pairs = [(i, i + by) for i in range(peers) if 0 <= i + by < peers]
    return lax.ppermute(x, axis, pairs)


def entering(x, axis, combine, identity):
    peers, place = (lax.axis_size(axis), lax.axis_index(axis))
    everything = jax.tree.map(lambda part: lax.all_gather(part, axis), x)
    start = jax.tree.map(
        lambda part, zero: jnp.broadcast_to(jnp.asarray(zero, part.dtype), part.shape), x, identity
    )

    def turn(k, before):
        reached = k < place
        new = combine(before, jax.tree.map(lambda part: part[k], everything))
        return jax.tree.map(lambda a, b: jnp.where(reached, a, b), new, before)

    return lax.fori_loop(0, peers, turn, start)


def causal_conv(prior_rows, raw_rows, conv_weight, conv_bias):
    joined = jnp.concatenate([prior_rows, raw_rows], axis=0).astype(jnp.float32)
    length = raw_rows.shape[0]
    running = jnp.broadcast_to(conv_bias[None, :], raw_rows.shape)
    for offset in range(conv_weight.shape[0]):
        running = running + conv_weight[offset][None, :] * joined[offset : offset + length]
    return jax.nn.silu(running).astype(jnp.bfloat16)


def combine_states(earlier, latter):
    return (earlier[0] * latter[0], latter[0][:, None, None] * earlier[1] + latter[1])


def body(
    hidden,
    in_weight,
    step_weight,
    group_weight,
    conv_inner,
    inner_bias,
    conv_group,
    group_bias,
    step_bias,
    log_rate,
    skip_weight,
    norm_gain,
    out_weight,
):
    heads_dev = log_rate.shape[0]
    inner_dev = in_weight.shape[2]
    group_cols = 2 * STATE
    group_index = lax.axis_index("tp") * heads_dev // (HEADS // GROUPS)
    zx_weight = in_weight.reshape(in_weight.shape[0], 2 * inner_dev)
    full_weight = lax.all_gather(group_weight, "tp", axis=0, tiled=True)
    map_weight = lax.dynamic_slice_in_dim(full_weight, group_index, 1, 1)[:, 0, :]
    shard_rows = lax.all_gather(hidden, "tp", axis=0, tiled=True)
    projected = jnp.concatenate(
        [
            jnp.dot(shard_rows, zx_weight, preferred_element_type=jnp.float32),
            lax.dot_general(
                shard_rows, map_weight, (((1,), (1,)), ((), ())), preferred_element_type=jnp.float32
            ),
            jnp.dot(shard_rows, step_weight, preferred_element_type=jnp.float32),
        ],
        axis=1,
    ).astype(jnp.bfloat16)
    gate_raw = projected[:, :inner_dev]
    inner_raw = projected[:, inner_dev : 2 * inner_dev]
    map_part = projected[:, 2 * inner_dev : projected.shape[1] - heads_dev]
    step_raw = projected[:, projected.shape[1] - heads_dev :]
    border_rows = KERNEL - 1
    length = inner_raw.shape[0]
    inner_prior, map_prior = shifted(
        (inner_raw[length - border_rows :], map_part[length - border_rows :]), "ctx", 1
    )
    x_conv = causal_conv(inner_prior, inner_raw, conv_inner, inner_bias)
    own_taps = lax.dynamic_slice_in_dim(conv_group, group_index * group_cols, group_cols, 1)
    own_bias = lax.dynamic_slice_in_dim(group_bias, group_index * group_cols, group_cols, 0)
    maps = causal_conv(map_prior, map_part, own_taps, own_bias)
    step_size = jax.nn.softplus(step_raw.astype(jnp.float32) + step_bias[None, :])
    decay_rate = -jnp.exp(log_rate)
    blocks = length // BLOCK
    x_blocks = x_conv.reshape(blocks, BLOCK, heads_dev, HEAD_DIM)
    input_map = maps[:, :STATE].reshape(blocks, BLOCK, STATE)
    output_map = maps[:, STATE:].reshape(blocks, BLOCK, STATE)
    step_blocks = jnp.swapaxes(step_size.reshape(blocks, BLOCK, heads_dev), 1, 2)
    cumulative = jnp.cumsum(step_blocks * decay_rate[None, :, None], axis=2)
    scores = jnp.einsum("kin,kjn->kij", output_map, input_map, preferred_element_type=jnp.float32)
    causal = jnp.arange(BLOCK)[:, None] >= jnp.arange(BLOCK)[None, :]
    exponent = jnp.where(causal, cumulative[..., :, None] - cumulative[..., None, :], -jnp.inf)
    mixing = (scores[:, None] * jnp.exp(exponent) * step_blocks[..., None, :]).astype(jnp.bfloat16)
    within = jnp.einsum("khij,kjhp->kihp", mixing, x_blocks, preferred_element_type=jnp.float32)
    weight = jnp.exp(cumulative[..., BLOCK - 1 :] - cumulative) * step_blocks
    x_float = x_blocks.astype(jnp.float32)
    weighted = (x_float * jnp.swapaxes(weight, 1, 2)[..., None]).astype(jnp.bfloat16)
    block_state = jnp.einsum(
        "kjhp,kjn->khpn", weighted, input_map, preferred_element_type=jnp.float32
    )
    block_decay = jnp.exp(cumulative[..., BLOCK - 1])

    def advance(carry, item):
        running, product = carry
        block_stop_index, state_here = item
        return (
            (block_stop_index[:, None, None] * running + state_here, product * block_stop_index),
            (running, product),
        )

    empty_state = jnp.zeros((heads_dev, HEAD_DIM, STATE), jnp.float32)
    (dev_state, dev_decay), (local_starts, prefixes) = lax.scan(
        advance, (empty_state, jnp.ones((heads_dev,), jnp.float32)), (block_decay, block_state)
    )
    decay_in, incoming = entering(
        (dev_decay, dev_state),
        "ctx",
        combine_states,
        (jnp.ones_like(dev_decay), jnp.zeros_like(dev_state)),
    )
    starting = local_starts + prefixes[:, :, None, None] * incoming[None]
    carried = jnp.einsum(
        "kin,khpn->kihp",
        output_map,
        starting.astype(jnp.bfloat16),
        preferred_element_type=jnp.float32,
    )
    carried = carried * jnp.swapaxes(jnp.exp(cumulative), 1, 2)[..., None]
    result_heads = within + carried + skip_weight[None, None, :, None] * x_float
    result_heads = result_heads.reshape(length, inner_dev)
    gated = result_heads * jax.nn.silu(gate_raw.astype(jnp.float32))
    squares = jnp.sum(gated * gated, axis=1)
    own_slot = (jnp.arange(GROUPS) == group_index)[:, None]
    group_sums = lax.psum(jnp.where(own_slot, squares[None, :], 0.0), "tp")
    own_total = jnp.sum(jnp.where(own_slot, group_sums, 0.0), axis=0)
    inverse = lax.rsqrt(own_total / (HEADS * HEAD_DIM // GROUPS) + 1e-05)
    normed = (gated * inverse[:, None] * norm_gain[None, :]).astype(jnp.bfloat16)
    mixed = lax.psum_scatter(
        jnp.dot(normed, out_weight, preferred_element_type=jnp.float32),
        "tp",
        scatter_dimension=0,
        tiled=True,
    )
    return mixed.astype(jnp.bfloat16)


def solution(mesh):
    placed = (
        P(("ctx", "tp"), None),
        P(None, None, "tp"),
        P(None, "tp"),
        P("tp", None, None),
        P(None, "tp"),
        P("tp"),
        P(),
        P(),
        P("tp"),
        P("tp"),
        P("tp"),
        P("tp"),
        P("tp", None),
    )
    return jax.shard_map(
        body, mesh=mesh, in_specs=placed, out_specs=P(("ctx", "tp"), None), check_vma=False
    )
```

profile of v0, /device:TPU:27, one launch (start us, length us, event | category | flops | bytes accessed | tf_op | source)
XLA Modules:
  0.0 323.9 jit_solution(4867282855328708421)
XLA Ops:
  7.3 1.8 copy.45
  9.3 2.1 copy.56
  13.1 41.7 %all-gather.6.cloned.1.call-done = bf16[256,2048]{1,0:T(8,128)(2,1)} async-done(((bf16[16,2048]{1,0:T(8,128)(2,1)}), bf16[256,2048]{1,0:T(8,128)(2,1)}) %all-gather.6.cloned.1.call-update) | async-done | bytes 1048592 | tf_op jit(solution)/shard_map/all_gather | solution.py:70
  54.8 1.6 bitcast_multiply_fusion.1
  56.4 1.2 reduce-window.6
  58.1 1.9 convolution_convert_fusion
  60.1 3.1 collective-permute-start
  64.4 35.8 %all-gather.8.cloned.1.call-done = bf16[256,4,2048]{2,0,1:T(8,128)(2,1)} async-done(((bf16[16,4,2048]{2,0,1:T(8,128)(2,1)}), bf16[256,4,2048]{2,0,1:T(8,128)(2,1)}) %all-gather.8.cloned.1.call-update) | async-done | bytes 4194320 | tf_op jit(solution)/shard_map/all_gather | solution.py:68
  100.3 2.0 fusion.4
  102.3 3.1 collective-permute-start.1
  107.9 34.2 %all-gather = f32[32,4,1]{1,2,0:T(1,128)S(1)} all-gather(f32[1,4,1]{1,2,0:T(1,128)S(1)} %copy.48), channel_id=2, replica_groups=mesh['ctx'=32,'tp'=16] {'ctx'}, dimensions={0}, use_global_device_ids=true | all-gather | bytes 528 | tf_op jit(solution)/shard_map/all_gather | solution.py:22
  142.6 49.1 %all-gather.10.cloned.1.call-done = f32[128,64,128]{2,1,0:T(8,128)} async-done(((f32[4,64,128]{2,1,0:T(8,128)}), f32[128,64,128]{2,1,0:T(8,128)}) %all-gather.10.cloned.1.call-update) | async-done | bytes 4194320 | tf_op jit(solution)/shard_map/all_gather | solution.py:22
  191.7 33.1 %while.9 = (s32[]{:T(128)}, f32[4,64,128]{2,1,0:T(8,128)S(1)}, s32[]{:T(128)}, f32[32,4]{1,0:T(8,128)S(1)}, f32[32,4,64,128]{3,2,1,0:T(8,128)}, /*index=5*/s32[]{:T(128)}, s32[]{:T(128)}) while((s32[]{:T(128)}, f32[4,64,128]{2,1,0:T(8,128)S(1)}, s32[]{:T(128)}, f32[32,4]{1,0:T(8,128)S(1)}, f32[32,4,64,128]{3,2,1,0:T(8,128)}, ...), condition=%wide.region_3.4_spmd.clone, body=%wide.region_2.3_spmd.clone.sunk | while | flops 131076 | bytes 393369 | solution.py:32
  192.7 1.0 fusion.52
  193.8 1.0 fusion.52
  194.8 1.0 fusion.52
  195.8 1.0 fusion.52
  196.9 1.0 fusion.52
  197.9 1.0 fusion.52
  198.9 1.0 fusion.52
  200.0 1.0 fusion.52
  201.0 1.0 fusion.52
  202.0 1.0 fusion.52
  203.1 1.0 fusion.52
  204.1 1.0 fusion.52
  205.1 1.0 fusion.52
  206.2 1.0 fusion.52
  207.2 1.0 fusion.52
  208.2 1.0 fusion.52
  209.3 1.0 fusion.52
  210.3 1.0 fusion.52
  211.3 1.0 fusion.52
  212.4 1.0 fusion.52
  213.4 1.0 fusion.52
  214.5 1.0 fusion.52
  215.5 1.0 fusion.52
  216.5 1.0 fusion.52
  217.6 1.0 fusion.52
  218.6 1.0 fusion.52
  219.6 1.0 fusion.52
  220.7 1.0 fusion.52
  221.7 1.0 fusion.52
  222.7 1.0 fusion.52
  223.8 1.0 fusion.52
  225.8 26.8 %psum.7 = f32[4,256]{1,0:T(4,128)S(1)} all-reduce(f32[4,256]{1,0:T(4,128)S(1)} %broadcast_select_fusion), channel_id=1, replica_groups=mesh['ctx'=32,'tp'=16] {'tp'}, use_global_device_ids=true, to_apply=%region_5.6 | all-reduce | flops 1024 | bytes 8192 | tf_op jit(solution)/shard_map/psum | solution.py:146
  252.8 1.8 fusion.27
  254.7 61.1 %reduce-scatter.2.cloned.1.call-done = f32[16,2048]{1,0:T(8,128)} async-done(((f32[256,2048]{1,0:T(8,128)}), f32[16,2048]{1,0:T(8,128)}) %reduce-scatter.2.cloned.1.call-update) | async-done | bytes 131088 | tf_op jit(solution)/shard_map/reduce_scatter | solution.py:150
  315.8 1.5 convert_element_type.77
  (103 shorter events, 9.5 us)
Async XLA Ops:
  6.5 246.2 %copy-start = (bf16[256,2048]{1,0:T(8,128)(2,1)S(1)}, bf16[256,2048]{1,0:T(8,128)(2,1)}, u32[]{:S(2)}) copy-start(bf16[256,2048]{1,0:T(8,128)(2,1)} %param.27) | copy-start | bytes 3145732
  6.5 48.3 %all-gather.6.cloned.1.call-start = ((), (), s32[]{:S(2)}) async-start(), calls=%async_computation.1 | async-start | bytes 1114112 | tf_op jit(solution)/shard_map/all_gather | solution.py:70
  7.3 93.0 %all-gather.8.cloned.1.call-start = ((), (), s32[]{:S(2)}) async-start(), calls=%async_computation.2 | async-start | bytes 4456448 | tf_op jit(solution)/shard_map/all_gather | solution.py:68
  9.2 182.5 %all-gather.10.cloned.1.call-start = ((), (), s32[]{:S(2)}) async-start(), calls=%async_computation.4 | async-start | bytes 4325376 | tf_op jit(solution)/shard_map/all_gather | solution.py:22
  9.2 3.8 %copy-start.5 = (f32[4]{0:T(128)S(1)}, f32[4]{0:T(128)}, u32[]{:S(2)}) copy-start(f32[4]{0:T(128)} %param.24) | copy-start | bytes 52
  9.2 3.8 %copy-start.1 = (f32[4,256]{1,0:T(4,128)S(1)}, f32[4,256]{1,0:T(4,128)}, u32[]{:S(2)}) copy-start(f32[4,256]{1,0:T(4,128)} %param.19) | copy-start | bytes 12292
  9.3 45.5 %copy-start.4 = (bf16[2048,4]{0,1:T(4,128)(2,1)S(1)}, bf16[2048,4]{0,1:T(4,128)(2,1)}, u32[]{:S(2)}) copy-start(bf16[2048,4]{0,1:T(4,128)(2,1)} %param.17) | copy-start | bytes 49156
  9.3 45.5 %copy-start.6 = (f32[4]{0:T(128)S(1)}, f32[4]{0:T(128)}, u32[]{:S(2)}) copy-start(f32[4]{0:T(128)} %param.23) | copy-start | bytes 52
  60.0 45.4 %copy-start.3 = (f32[256]{0:T(256)S(1)}, f32[256]{0:T(256)}, u32[]{:S(2)}) copy-start(f32[256]{0:T(256)} %param.20) | copy-start | bytes 3076
  60.1 4.3 %collective-permute-start = (bf16[3,256]{1,0:T(4,128)(2,1)S(1)}, bf16[3,256]{1,0:T(4,128)(2,1)S(1)}, u32[]{:S(2)}, u32[]{:S(2)}) collective-permute-start(bf16[3,256]{1,0:T(4,128)(2,1)S(1)} %slice.112), channel_id=1, source_target_pairs={{0,16},{16,32},{32,48},{48,64},{64,80},{80,96},{96,112},{112,128},... | collective-permute-start | bytes 4616 | tf_op jit(solution)/shard_map/ppermute | solution.py:17
  102.3 4.3 %collective-permute-start.1 = (bf16[3,256]{1,0:T(4,128)(2,1)S(1)}, bf16[3,256]{1,0:T(4,128)(2,1)S(1)}, u32[]{:S(2)}, u32[]{:S(2)}) collective-permute-start(bf16[3,256]{1,0:T(4,128)(2,1)S(1)} %slice.118), channel_id=1, source_target_pairs={{0,16},{16,32},{32,48},{48,64},{64,80},{80,96},{96,112},{112,128},... | collective-permute-start | bytes 4616 | tf_op jit(solution)/shard_map/ppermute | solution.py:17
  106.8 118.1 %copy-start.7 = (f32[4]{0:T(128)S(1)}, f32[4]{0:T(128)}, u32[]{:S(2)}) copy-start(f32[4]{0:T(128)} %param.25) | copy-start | bytes 52
  107.7 208.1 %reduce-scatter.2.cloned.1.call-start = ((), (), s32[]{:S(2)}) async-start(), calls=%async_computation.3 | async-start | bytes 2228224 | tf_op jit(solution)/shard_map/reduce_scatter | solution.py:150
  224.8 28.0 %copy-start.2 = (f32[256]{0:T(256)S(1)}, f32[256]{0:T(256)}, u32[]{:S(2)}) copy-start(f32[256]{0:T(256)} %param.26) | copy-start | bytes 3076
Sparse Core Ops, SparseCore 0:
  9.5 45.2 all-gather.5
  56.9 43.2 all-gather.7
  107.8 83.8 all-gather.9
  254.8 60.9 reduce-scatter.1
where the time goes:
time: 325 us; the launch traced here: 324 us
  waiting for transfers between devices  190 us (58%)
  blocking collectives  61.1 us (19%)
  other arithmetic  35.5 us (11%)
  between operations  13.5 us (4%)
  matrix products  9.08 us (3%)
  local copies, waits for them, and re-layouts  7.25 us (2%)
  starting transfers between devices  6.32 us (2%)
    reduce_scatter x1, waiting for transfers between devices, body(): lax.psum_scatter(jnp.dot(normed, out_weight, preferred_element_type=jnp.f...  61.1 us
    all_gather x1, waiting for transfers between devices, entering(): everything = jax.tree.map(lambda part: lax.all_gather(part, axis), x)  49.1 us
    all_gather x1, waiting for transfers between devices, body(): shard_rows = lax.all_gather(hidden, 'tp', axis=0, tiled=True)  41.7 us
    all_gather x1, waiting for transfers between devices, body(): full_weight = lax.all_gather(group_weight, 'tp', axis=0, tiled=True)  35.8 us
    all_gather x1, blocking collectives, entering(): everything = jax.tree.map(lambda part: lax.all_gather(part, axis), x)  34.2 us
    select_n x32, other arithmetic, turn(): return jax.tree.map(lambda a, b: jnp.where(reached, a, b), new, before)  31.8 us
    psum x1, blocking collectives, body(): group_sums = lax.psum(jnp.where(own_slot, squares[None, :], 0.0), 'tp')  26.8 us
  transfers between devices with their start and end apart: 6, of which 6 were waited for; matrix products, arithmetic and copies ran while one was open for 4% of the time, Pallas kernels for 0%

commit v1 on v0

--- a/solution.py
+++ b/solution.py
@@ -2,6 +2,7 @@
 import jax.numpy as jnp
 from jax import lax
 from jax.sharding import PartitionSpec as P
+from jax.lax import all_gather
 
 HEADS = 64
 HEAD_DIM = 64
@@ -9,6 +10,7 @@
 GROUPS = 4
 BLOCK = 256
 KERNEL = 4
+run_edges = lambda here_x, peer_axis: jnp.sum(all_gather(here_x, axis_name=peer_axis), axis=0)
 
 
 def shifted(x, axis, by):
@@ -143,7 +145,7 @@
     gated = result_heads * jax.nn.silu(gate_raw.astype(jnp.float32))
     squares = jnp.sum(gated * gated, axis=1)
     own_slot = (jnp.arange(GROUPS) == group_index)[:, None]
-    group_sums = lax.psum(jnp.where(own_slot, squares[None, :], 0.0), "tp")
+    group_sums = run_edges(jnp.where(own_slot, squares[None, :], 0.0), "tp")
     own_total = jnp.sum(jnp.where(own_slot, group_sums, 0.0), axis=0)
     inverse = lax.rsqrt(own_total / (HEADS * HEAD_DIM // GROUPS) + 1e-05)
     normed = (gated * inverse[:, None] * norm_gain[None, :]).astype(jnp.bfloat16)

time: 325 us -> 316 us (0.972)
  the two profiles are of different devices: /device:TPU:27 before, /device:TPU:25 now
where the time goes in v1:
time: 316 us; the launch traced here: 315 us
  waiting for transfers between devices  188 us (59%)
  blocking collectives  55 us (17%)
  other arithmetic  35.5 us (11%)
  between operations  13.5 us (4%)
  matrix products  9.07 us (3%)
  local copies, waits for them, and re-layouts  7.25 us (2%)
  starting transfers between devices  6.31 us (2%)
    reduce_scatter x1, waiting for transfers between devices, body(): lax.psum_scatter(jnp.dot(normed, out_weight, preferred_element_type=jnp.f...  57.9 us
    all_gather x1, waiting for transfers between devices, entering(): everything = jax.tree.map(lambda part: lax.all_gather(part, axis), x)  50.2 us
    all_gather x1, waiting for transfers between devices, body(): shard_rows = lax.all_gather(hidden, 'tp', axis=0, tiled=True)  41.8 us
    all_gather x1, waiting for transfers between devices, body(): full_weight = lax.all_gather(group_weight, 'tp', axis=0, tiled=True)  36.4 us
    all_gather x1, blocking collectives, entering(): everything = jax.tree.map(lambda part: lax.all_gather(part, axis), x)  35 us
    select_n x32, other arithmetic, turn(): return jax.tree.map(lambda a, b: jnp.where(reached, a, b), new, before)  31.8 us
    all_gather x1, blocking collectives, all_gather(here_x, axis_name=peer_axis)  19.9 us
  transfers between devices with their start and end apart: 6, of which 6 were waited for; matrix products, arithmetic and copies ran while one was open for 4% of the time, Pallas kernels for 0%

profile of v1, /device:TPU:25, one launch (start us, length us, event | category | flops | bytes accessed | tf_op | source)
XLA Modules:
  0.0 315.1 jit_solution(14342866990122628371)
XLA Ops:
  7.3 1.8 copy.45
  9.3 2.1 copy.56
  13.1 41.8 %all-gather.6.cloned.1.call-done = bf16[256,2048]{1,0:T(8,128)(2,1)} async-done(((bf16[16,2048]{1,0:T(8,128)(2,1)}), bf16[256,2048]{1,0:T(8,128)(2,1)}) %all-gather.6.cloned.1.call-update) | async-done | bytes 1048592 | tf_op jit(solution)/shard_map/all_gather | solution.py:72
  54.8 1.6 bitcast_multiply_fusion.1
  56.5 1.2 reduce-window.6
  58.1 1.9 convolution_convert_fusion
  60.1 3.1 collective-permute-start
  63.9 36.4 %all-gather.8.cloned.1.call-done = bf16[256,4,2048]{2,0,1:T(8,128)(2,1)} async-done(((bf16[16,4,2048]{2,0,1:T(8,128)(2,1)}), bf16[256,4,2048]{2,0,1:T(8,128)(2,1)}) %all-gather.8.cloned.1.call-update) | async-done | bytes 4194320 | tf_op jit(solution)/shard_map/all_gather | solution.py:70
  100.3 2.0 fusion.4
  102.3 3.1 collective-permute-start.1
  107.4 35.0 %all-gather = f32[32,4,1]{1,2,0:T(1,128)S(1)} all-gather(f32[1,4,1]{1,2,0:T(1,128)S(1)} %copy.48), channel_id=2, replica_groups=mesh['ctx'=32,'tp'=16] {'ctx'}, dimensions={0}, use_global_device_ids=true | all-gather | bytes 528 | tf_op jit(solution)/shard_map/all_gather | solution.py:24
  142.9 50.2 %all-gather.10.cloned.1.call-done = f32[128,64,128]{2,1,0:T(8,128)} async-done(((f32[4,64,128]{2,1,0:T(8,128)}), f32[128,64,128]{2,1,0:T(8,128)}) %all-gather.10.cloned.1.call-update) | async-done | bytes 4194320 | tf_op jit(solution)/shard_map/all_gather | solution.py:24
  193.1 33.1 %while.9 = (s32[]{:T(128)}, f32[4,64,128]{2,1,0:T(8,128)S(1)}, s32[]{:T(128)}, f32[32,4]{1,0:T(8,128)S(1)}, f32[32,4,64,128]{3,2,1,0:T(8,128)}, /*index=5*/s32[]{:T(128)}, s32[]{:T(128)}) while((s32[]{:T(128)}, f32[4,64,128]{2,1,0:T(8,128)S(1)}, s32[]{:T(128)}, f32[32,4]{1,0:T(8,128)S(1)}, f32[32,4,64,128]{3,2,1,0:T(8,128)}, ...), condition=%wide.region_3.4_spmd.clone, body=%wide.region_2.3_spmd.clone.sunk | while | flops 131076 | bytes 393369 | solution.py:34
  194.1 1.0 fusion.52
  195.1 1.0 fusion.52
  196.2 1.0 fusion.52
  197.2 1.0 fusion.52
  198.3 1.0 fusion.52
  199.3 1.0 fusion.52
  200.3 1.0 fusion.52
  201.4 1.0 fusion.52
  202.4 1.0 fusion.52
  203.4 1.0 fusion.52
  204.5 1.0 fusion.52
  205.5 1.0 fusion.52
  206.5 1.0 fusion.52
  207.6 1.0 fusion.52
  208.6 1.0 fusion.52
  209.6 1.0 fusion.52
  210.7 1.0 fusion.52
  211.7 1.0 fusion.52
  212.7 1.0 fusion.52
  213.8 1.0 fusion.52
  214.8 1.0 fusion.52
  215.8 1.0 fusion.52
  216.9 1.0 fusion.52
  217.9 1.0 fusion.52
  218.9 1.0 fusion.52
  220.0 1.0 fusion.52
  221.0 1.0 fusion.52
  222.0 1.0 fusion.52
  223.1 1.0 fusion.52
  224.1 1.0 fusion.52
  225.1 1.0 fusion.52
  227.2 19.9 %all_gather.22 = f32[16,4,256]{2,1,0:T(4,128)S(1)} all-gather(f32[1,4,256]{2,1,0:T(4,128)S(1)} %broadcast_select_fusion), channel_id=1, replica_groups=mesh['ctx'=32,'tp'=16] {'tp'}, dimensions={0}, use_global_device_ids=true | all-gather | bytes 69632 | tf_op jit(solution)/shard_map/all_gather | solution.py:13
  247.3 1.8 fusion.27
  249.2 57.9 %reduce-scatter.2.cloned.1.call-done = f32[16,2048]{1,0:T(8,128)} async-done(((f32[256,2048]{1,0:T(8,128)}), f32[16,2048]{1,0:T(8,128)}) %reduce-scatter.2.cloned.1.call-update) | async-done | bytes 131088 | tf_op jit(solution)/shard_map/reduce_scatter | solution.py:152
  307.0 1.5 convert_element_type.77
  (104 shorter events, 8.5 us)
Async XLA Ops:
  6.5 240.8 %copy-start = (bf16[256,2048]{1,0:T(8,128)(2,1)S(1)}, bf16[256,2048]{1,0:T(8,128)(2,1)}, u32[]{:S(2)}) copy-start(bf16[256,2048]{1,0:T(8,128)(2,1)} %param.27) | copy-start | bytes 3145732
  6.5 48.3 %all-gather.6.cloned.1.call-start = ((), (), s32[]{:S(2)}) async-start(), calls=%async_computation.1 | async-start | bytes 1114112 | tf_op jit(solution)/shard_map/all_gather | solution.py:72
  7.3 93.0 %all-gather.8.cloned.1.call-start = ((), (), s32[]{:S(2)}) async-start(), calls=%async_computation.2 | async-start | bytes 4456448 | tf_op jit(solution)/shard_map/all_gather | solution.py:70
  9.2 183.9 %all-gather.10.cloned.1.call-start = ((), (), s32[]{:S(2)}) async-start(), calls=%async_computation.4 | async-start | bytes 4325376 | tf_op jit(solution)/shard_map/all_gather | solution.py:24
  9.2 3.8 %copy-start.5 = (f32[4]{0:T(128)S(1)}, f32[4]{0:T(128)}, u32[]{:S(2)}) copy-start(f32[4]{0:T(128)} %param.24) | copy-start | bytes 52
  9.2 3.8 %copy-start.1 = (f32[4,256]{1,0:T(4,128)S(1)}, f32[4,256]{1,0:T(4,128)}, u32[]{:S(2)}) copy-start(f32[4,256]{1,0:T(4,128)} %param.19) | copy-start | bytes 12292
  9.3 45.6 %copy-start.4 = (bf16[2048,4]{0,1:T(4,128)(2,1)S(1)}, bf16[2048,4]{0,1:T(4,128)(2,1)}, u32[]{:S(2)}) copy-start(bf16[2048,4]{0,1:T(4,128)(2,1)} %param.17) | copy-start | bytes 49156
  9.3 45.6 %copy-start.6 = (f32[4]{0:T(128)S(1)}, f32[4]{0:T(128)}, u32[]{:S(2)}) copy-start(f32[4]{0:T(128)} %param.23) | copy-start | bytes 52
  60.0 45.4 %copy-start.3 = (f32[256]{0:T(256)S(1)}, f32[256]{0:T(256)}, u32[]{:S(2)}) copy-start(f32[256]{0:T(256)} %param.20) | copy-start | bytes 3076
  60.1 3.8 %collective-permute-start = (bf16[3,256]{1,0:T(4,128)(2,1)S(1)}, bf16[3,256]{1,0:T(4,128)(2,1)S(1)}, u32[]{:S(2)}, u32[]{:S(2)}) collective-permute-start(bf16[3,256]{1,0:T(4,128)(2,1)S(1)} %slice.112), channel_id=1, source_target_pairs={{0,16},{16,32},{32,48},{48,64},{64,80},{80,96},{96,112},{112,128},... | collective-permute-start | bytes 4616 | tf_op jit(solution)/shard_map/ppermute | solution.py:19
  102.3 3.8 %collective-permute-start.1 = (bf16[3,256]{1,0:T(4,128)(2,1)S(1)}, bf16[3,256]{1,0:T(4,128)(2,1)S(1)}, u32[]{:S(2)}, u32[]{:S(2)}) collective-permute-start(bf16[3,256]{1,0:T(4,128)(2,1)S(1)} %slice.118), channel_id=1, source_target_pairs={{0,16},{16,32},{32,48},{48,64},{64,80},{80,96},{96,112},{112,128},... | collective-permute-start | bytes 4616 | tf_op jit(solution)/shard_map/ppermute | solution.py:19
  106.3 120.0 %copy-start.7 = (f32[4]{0:T(128)S(1)}, f32[4]{0:T(128)}, u32[]{:S(2)}) copy-start(f32[4]{0:T(128)} %param.25) | copy-start | bytes 52
  107.2 199.8 %reduce-scatter.2.cloned.1.call-start = ((), (), s32[]{:S(2)}) async-start(), calls=%async_computation.3 | async-start | bytes 2228224 | tf_op jit(solution)/shard_map/reduce_scatter | solution.py:152
  226.1 21.2 %copy-start.2 = (f32[256]{0:T(256)S(1)}, f32[256]{0:T(256)}, u32[]{:S(2)}) copy-start(f32[256]{0:T(256)} %param.26) | copy-start | bytes 3076
Sparse Core Ops, SparseCore 0:
  9.5 45.3 all-gather.5
  57.0 43.2 all-gather.7
  107.3 85.7 all-gather.9
  249.3 57.6 reduce-scatter.1
